TPU v7x, 128 devices: a whole 4x4x4 slice. The times are simulated.
128 devices in a mesh: req: 4 (over y), exp: 32 (over z, x, core).
Axes of the slice: x: 4, y: 4, z: 4, core: 2. Of those that a mesh axis runs over, the one named last changes fastest.
Arguments:
- states: bfloat16 [2, 16384, 1024], P(None, ('req', 'exp')), may hold values from -6 to 6
- lengths: int32 [128, 4], P(('req', 'exp')), may hold values from 1 to 64, 128 in all within a row
- targets: int32 [16384], P('req'), may hold values from 0 to 36863
- routes: int32 [2, 16384, 8], P(None, ('req', 'exp')), may hold values from 0 to 31, all different within a row; in each aligned block of 128 rows (0 to 127, 128 to 255, ..., all dimensions but the last counted through in order) at most 40 rows name the same one
- gate_probs: float32 [2, 16384, 8], P(None, ('req', 'exp')), may hold values from 0.02 to 0.4
- owners: int32 [512], P(('req', 'exp')), may hold values from 0 to 511, each once
- norm_gains: float32 [2, 3, 1024], replicated, may hold values from 0.25 to 1.75
- qkv_weight: bfloat16 [2, 1024, 2048], replicated, may hold values from -14 to 14
- out_weight: bfloat16 [2, 1024, 1024], replicated, may hold values from -0.1875 to 0.1875
- expert_in: bfloat16 [2, 32, 1024, 1024], P(None, 'exp'), may hold values from -0.1875 to 0.1875
- expert_down: bfloat16 [2, 32, 512, 1024], P(None, 'exp'), may hold values from -0.25 to 0.25
- vocab_head: bfloat16 [2, 36864, 1024], P(None, 'exp'), may hold values from -170 to 170
Outputs:
- token_logp: float32 [2, 16384], P(None, ('req', 'exp'))
- seq_totals: float32 [512], P(('req', 'exp'))
Inputs may be any that keep to these rules, and one draw needn't show every extreme that they name: `lengths`: each row sums to 128; some row reaches 64. `routes`: the 8 experts of a token are distinct; among the 128 tokens of one device, no expert is named by more than 40 of them for one model, and that bound is reached. `owners`: a permutation of the sequence numbers.
All inputs are finite; a program needn't handle non-finite values.
Results may differ from a plain program's by a relative error of at most 0.012.
The roundings to bfloat16 on the way count: a program that leaves them out, or rounds other values in their place, can miss the bound.
Values may be sent and summed in bfloat16 or wider, within the bound.
No kernel may reach another device: no remote copies, remote signals or barrier semaphores. Data moves between devices by JAX's collectives and lax.ppermute only.
A program may use at most 128 MiB of HBM per device.

v0:
```python
import jax
import jax.numpy as jnp
from jax import lax
from jax.sharding import PartitionSpec as P

HEADS = 16
KV_HEADS = 8
HEAD_DIM = 64
EXPERT_FF = 512
EXPERTS = 32
TOP = 8
CAP = 40
EPSILON = 1e-06
RESIDUAL_SCALE = 0.22
SCORE_SCALE = 0.015625
LOGIT_DIVISOR = 6.0
ROTARY_BASE = 10000.0


def combined_all(x, axis, combine):
    everything = jax.tree.map(lambda part: lax.all_gather(part, axis), x)
    initial = jax.tree.map(lambda part: part[0], everything)

    def step(k, so_far):
        return combine(so_far, jax.tree.map(lambda part: part[k], everything))

    return lax.fori_loop(1, lax.axis_size(axis), step, initial)


def root_norm(values, gain_row):
    values = values.astype(jnp.float32)
    scaled = lax.rsqrt(jnp.mean(values * values, axis=-1, keepdims=True) + EPSILON)
    return values * scaled * gain_row


def segment_table(length_row, token_count):
    seq_ends = jnp.cumsum(length_row)
    seq_starts = seq_ends - length_row
    places = jnp.arange(token_count, dtype=jnp.int32)
    segment = jnp.sum((places[:, None] >= seq_ends[None, :]).astype(jnp.int32), axis=1)
    member = segment[:, None] == jnp.arange(length_row.shape[0], dtype=jnp.int32)[None, :]
    position = places - jnp.sum(member.astype(jnp.int32) * seq_starts[None, :], axis=1)
    return (segment, member, position)


def rotary(values, position):
    half_dim = values.shape[-1] // 2
    frequency = ROTARY_BASE ** (-2.0 * jnp.arange(half_dim, dtype=jnp.float32) / values.shape[-1])
    angles = position.astype(jnp.float32)[:, None] * frequency[None, :]
    angles = jnp.concatenate([angles, angles], axis=-1)[:, None, :]
    leading = values[..., :half_dim]
    trailing = values[..., half_dim:]
    turned = jnp.concatenate([-trailing, leading], axis=-1)
    return values * jnp.cos(angles) + turned * jnp.sin(angles)


def attend(block_states, segment, position, gain_row, qkv_weight, out_weight):
    token_count = block_states.shape[0]
    group_size = HEADS // KV_HEADS
    normed = root_norm(block_states, gain_row).astype(jnp.bfloat16)
    mixed = jnp.dot(normed, qkv_weight, preferred_element_type=jnp.float32)
    queries = rotary(
        mixed[:, : HEADS * HEAD_DIM].reshape(token_count, HEADS, HEAD_DIM), position
    ).astype(jnp.bfloat16)
    keys_all = rotary(
        mixed[:, HEADS * HEAD_DIM : (HEADS + KV_HEADS) * HEAD_DIM].reshape(
            token_count, KV_HEADS, HEAD_DIM
        ),
        position,
    ).astype(jnp.bfloat16)
    values_all = (
        mixed[:, (HEADS + KV_HEADS) * HEAD_DIM :]
        .reshape(token_count, KV_HEADS, HEAD_DIM)
        .astype(jnp.bfloat16)
    )
    grouped = queries.reshape(token_count, KV_HEADS, group_size, HEAD_DIM)
    scores = (
        jnp.einsum("tgqd,sgd->gqts", grouped, keys_all, preferred_element_type=jnp.float32)
        * SCORE_SCALE
    )
    places = jnp.arange(token_count, dtype=jnp.int32)
    allowed = (segment[:, None] == segment[None, :]) & (places[None, :] <= places[:, None])
    scores = jnp.where(allowed, scores, -1e30)
    highest = jnp.max(scores, axis=-1, keepdims=True)
    weights = jnp.exp(scores - highest)
    weights = (weights / jnp.sum(weights, axis=-1, keepdims=True)).astype(jnp.bfloat16)
    attended = jnp.einsum(
        "gqts,sgd->tgqd", weights, values_all, preferred_element_type=jnp.float32
    ).astype(jnp.bfloat16)
    projected = jnp.dot(
        attended.reshape(token_count, HEADS * HEAD_DIM),
        out_weight,
        preferred_element_type=jnp.float32,
    )
    return (block_states.astype(jnp.float32) + RESIDUAL_SCALE * projected).astype(jnp.bfloat16)


def join_parts(first_part, second_part):
    first_max, first_mass, first_hit = first_part
    second_max, second_mass, second_hit = second_part
    joined_max = jnp.maximum(first_max, second_max)
    joined_mass = first_mass * jnp.exp(first_max - joined_max) + second_mass * jnp.exp(
        second_max - joined_max
    )
    return (joined_max, joined_mass, first_hit + second_hit)


def per_device(
    states,
    lengths,
    targets,
    routes,
    gate_probs,
    owners,
    norm_gains,
    qkv_weight,
    out_weight,
    expert_in,
    expert_down,
    vocab_head,
):
    token_count = states.shape[1]
    width = states.shape[2]
    segment, member, position = segment_table(lengths[0], token_count)
    residual = jnp.stack(
        [
            attend(
                states[which],
                segment,
                position,
                norm_gains[which, 0],
                qkv_weight[which],
                out_weight[which],
            )
            for which in range(2)
        ]
    )
    moe_in = root_norm(residual, norm_gains[:, 1][:, None, :]).astype(jnp.bfloat16)
    groups = lax.axis_size("exp")
    local_count = expert_in.shape[1]
    flat_routes = routes.reshape(2, token_count * TOP)
    onehot = (flat_routes[..., None] == jnp.arange(EXPERTS, dtype=jnp.int32)).astype(jnp.int32)
    rank_slot = jnp.sum((jnp.cumsum(onehot, axis=1) - 1) * onehot, axis=2)
    slot_index = (
        flat_routes * CAP + rank_slot + jnp.arange(2, dtype=jnp.int32)[:, None] * (EXPERTS * CAP)
    ).reshape(-1)
    token_index = jnp.arange(token_count * TOP, dtype=jnp.int32) // TOP
    outgoing = (
        jnp.zeros((2 * EXPERTS * CAP, width), jnp.bfloat16)
        .at[slot_index]
        .set(moe_in[:, token_index].reshape(-1, width))
    )
    arrived = lax.all_to_all(
        outgoing.reshape(2, groups, local_count * CAP, width),
        "exp",
        split_axis=1,
        concat_axis=1,
        tiled=True,
    )
    inputs = arrived.reshape(2, groups, local_count, CAP, width)
    gate_up = jnp.einsum("mslcd,mldf->mslcf", inputs, expert_in, preferred_element_type=jnp.float32)
    hidden = (jax.nn.silu(gate_up[..., :EXPERT_FF]) * gate_up[..., EXPERT_FF:]).astype(jnp.bfloat16)
    produced = jnp.einsum(
        "mslcf,mlfd->mslcd", hidden, expert_down, preferred_element_type=jnp.float32
    ).astype(jnp.bfloat16)
    returned = lax.all_to_all(
        produced.reshape(2, groups, local_count * CAP, width),
        "exp",
        split_axis=1,
        concat_axis=1,
        tiled=True,
    )
    picked = returned.reshape(2 * EXPERTS * CAP, width)[slot_index].reshape(
        2, token_count, TOP, width
    )
    mixture = jnp.sum(gate_probs[..., None] * picked.astype(jnp.float32), axis=2)
    final = root_norm(
        residual.astype(jnp.float32) + RESIDUAL_SCALE * mixture, norm_gains[:, 2][:, None, :]
    ).astype(jnp.bfloat16)
    shard = lax.axis_index("exp")
    vocab_rows = vocab_head.shape[1]
    lowest = shard * vocab_rows
    vocab_ids = jnp.arange(vocab_rows, dtype=jnp.int32)
    shard_piece = lax.all_gather(final, "exp", axis=1, tiled=True)
    piece_rows = shard_piece.shape[1]
    block_rows = 512
    block_count = piece_rows // block_rows
    wanted_all = targets - lowest

    def one_block(block_number):
        row_block = lax.dynamic_slice_in_dim(shard_piece, block_number * block_rows, block_rows, 1)
        wanted = lax.dynamic_slice_in_dim(wanted_all, block_number * block_rows, block_rows, 0)
        logits = (
            jnp.einsum("mtd,mvd->mtv", row_block, vocab_head, preferred_element_type=jnp.float32)
            / LOGIT_DIVISOR
        )
        highest = jnp.max(logits, axis=2)
        masses = jnp.sum(jnp.exp(logits - highest[..., None]), axis=2)
        chosen = jnp.sum(
            jnp.where(wanted[None, :, None] == vocab_ids[None, None, :], logits, 0.0), axis=2
        )
        return (highest, masses, chosen)

    block_max, block_mass, block_hit = lax.map(one_block, jnp.arange(block_count, dtype=jnp.int32))

    def place(fresh):
        ordered = jnp.transpose(fresh, (1, 0, 2)).reshape(2, piece_rows)
        return ordered

    part_max = place(block_max)
    part_mass = place(block_mass)
    part_hit = place(block_hit)
    all_max, all_mass, all_hit = combined_all((part_max, part_mass, part_hit), "exp", join_parts)
    begin = shard * token_count
    final_max = lax.dynamic_slice_in_dim(all_max, begin, token_count, 1)
    final_mass = lax.dynamic_slice_in_dim(all_mass, begin, token_count, 1)
    final_hit = lax.dynamic_slice_in_dim(all_hit, begin, token_count, 1)
    token_logp = final_hit - (final_max + jnp.log(final_mass))
    difference = token_logp[0] - token_logp[1]
    seq_sums = jnp.sum(member.astype(jnp.float32) * difference[:, None], axis=0)
    devices = lax.axis_size("req") * lax.axis_size("exp")
    everyone = devices * seq_sums.shape[0]
    dense_totals = jnp.sum(
        (owners[:, None] == jnp.arange(everyone, dtype=jnp.int32)[None, :]).astype(jnp.float32)
        * seq_sums[:, None],
        axis=0,
    )
    seq_totals = lax.psum_scatter(dense_totals, ("req", "exp"), scatter_dimension=0, tiled=True)
    return (token_logp, seq_totals)


def solution(mesh):
    in_specs = (
        P(None, ("req", "exp"), None),
        P(("req", "exp"), None),
        P("req"),
        P(None, ("req", "exp"), None),
        P(None, ("req", "exp"), None),
        P(("req", "exp")),
        P(),
        P(),
        P(),
        P(None, "exp", None, None),
        P(None, "exp", None, None),
        P(None, "exp", None),
    )
    out_specs = (P(None, ("req", "exp")), P(("req", "exp")))
    return jax.shard_map(
        per_device, mesh=mesh, in_specs=in_specs, out_specs=out_specs, check_vma=False
    )
```

profile of v0, /device:TPU:1, one launch (start us, length us, event | category | flops | bytes accessed | tf_op | source)
XLA Modules:
  0.0 671.6 jit_solution(7500306601122006520)
XLA Ops:
  7.2 1.4 fusion.72
  9.4 3.1 fusion.15
  12.5 1.0 copy-done.2
  15.6 2.3 fusion.42
  17.9 2.1 fusion.144
  20.0 1.6 slice.227
  21.6 3.1 fusion.13
  24.7 0.9 copy-done.3
  26.8 2.4 fusion.40
  29.2 2.1 fusion.139
  31.3 1.0 slice.226
  35.6 1.0 copy.109
  36.7 2.7 convolution_convert_fusion.2
  39.4 2.2 fusion.61
  41.6 2.8 convolution_convert_fusion.1
  44.4 2.2 fusion.64
  47.5 15.8 %gather_fusion = bf16[1024,2,1024]{2,1,0:T(2,128)(2,1)} fusion(bf16[2,128,1024]{2,0,1:T(2,128)(2,1)S(1)} %copy.125, s32[1024]{0:T(1024)S(1)} %broadcast_clamp_fusion.1), kind=kCustom, calls=%fused_computation | custom fusion | bytes 8392704 | tf_op jit(solution)/shard_map/gather | solution.py:151
  63.3 5.6 copy.126
  68.9 18.0 %reduce-window.11 = s32[2,32,8,128]{3,2,1,0:T(8,128)S(1)} reduce-window(s32[2,32,8,128]{3,2,1,0:T(8,128)S(1)} %fusion.101, s32[]{:T(128)} %constant.119.clone.1), window={size=1x1x1x128 pad=0_0x0_0x0_0x127_0}, to_apply=%region_9.10 | reduce-window | flops 8323072 | bytes 524292 | tf_op jit(solution)/shard_map/reduce-window.1
  88.0 13.6 %scatter_custom_fusion = bf16[2560,1024]{1,0:T(8,128)(2,1)} fusion(s32[2048]{0:T(1024)S(1)} %bitcast.262, bf16[2048,1024]{1,0:T(8,128)(2,1)} %bitcast.240, bf16[]{:T(256)} %constant.129.clone.1), kind=kCustom, calls=%fused_computation.37 | custom fusion | bytes 5243392 | tf_op jit(solution)/shard_map/scatter | solution.py:151
  101.7 3.3 copy.127
  105.0 71.5 %all_to_all.10 = bf16[2,32,40,1024]{3,2,0,1:T(8,128)(2,1)S(1)} all-to-all(bf16[2,32,40,1024]{3,2,0,1:T(8,128)(2,1)S(1)} %copy.127), channel_id=1, replica_groups=mesh['req'=4,'exp'=32] {'exp'}, dimensions={1} | all-to-all | bytes 10485760 | tf_op jit(solution)/shard_map/all_to_all | solution.py:153
  176.5 8.2 %fusion.19 = f32[2,32,1,40,1024]{4,3,1,0,2:T(8,128)} fusion(bf16[2,1,1024,1024]{3,2,1,0:T(8,128)(2,1)S(1)} %copy-done.20, bf16[2,32,40,1024]{3,2,0,1:T(8,128)(2,1)S(1)} %all_to_all.10), kind=kOutput, calls=%fused_computation.34 | convolution fusion | flops 5368709120 | bytes 19922944 | tf_op jit(solution)/shard_map/mslcd,mldf->mslcf/dot_general | solution.py:161
  184.7 7.2 %convolution_convert_fusion = bf16[2,32,40,1024]{3,2,1,0:T(8,128)(2,1)S(1)} fusion(f32[2,32,1,40,1024]{4,3,1,0,2:T(8,128)} %fusion.19, bf16[2,1,512,1024]{3,2,1,0:T(8,128)(2,1)S(1)} %copy-done), kind=kOutput, calls=%fused_computation.35 | convolution fusion | flops 2694840320 | bytes 17825792 | tf_op jit(solution)/shard_map/mslcf,mlfd->mslcd/dot_general | solution.py:163
  191.8 3.2 copy.129
  195.0 5.0 all-to-all-start.1
  200.2 61.7 %all-to-all-done.1 = bf16[2,32,40,1024]{3,2,0,1:T(8,128)(2,1)} async-done(((bf16[2,32,40,1024]{3,2,0,1:T(8,128)(2,1)}), bf16[2,32,40,1024]{3,2,0,1:T(8,128)(2,1)}, u32[]{:S(2)}, u32[]{:S(2)}) %all-to-all-start.1) | async-done | bytes 5242912 | tf_op jit(solution)/shard_map/all_to_all | solution.py:166
  261.9 5.6 copy.130
  267.5 14.1 %gather_fusion.1 = bf16[2048,1024]{1,0:T(8,128)(2,1)} fusion(bf16[2560,1024]{1,0:T(8,128)(2,1)} %bitcast.231, s32[2048]{0:T(1024)S(1)} %broadcast_clamp_fusion), kind=kCustom, calls=%fused_computation.1 | custom fusion | bytes 8396800 | tf_op jit(solution)/shard_map/gather | solution.py:173
  281.6 4.8 fusion.8
  286.7 1.0 multiply_convert_fusion
  287.8 73.6 %all-gather.5.cloned.1.call-done = bf16[2,4096,1024]{2,1,0:T(8,128)(2,1)} async-done(((bf16[2,128,1024]{2,1,0:T(8,128)(2,1)}), bf16[2,4096,1024]{2,1,0:T(8,128)(2,1)}) %all-gather.5.cloned.1.call-update) | async-done | bytes 16777232 | tf_op jit(solution)/shard_map/all_gather | solution.py:184
  361.4 79.6 %while.35 = (s32[]{:T(128)}, f32[8,2,512]{2,1,0:T(2,128)S(1)}, f32[8,2,512]{2,1,0:T(2,128)}, f32[8,2,512]{2,1,0:T(2,128)}, s32[8]{0:T(128)S(1)}, /*index=5*/bf16...) while((s32[]{:T(128)}, f32[8,2,512]{2,1,0:T(2,128)S(1)}, ...), condition=%wide.region_20.21_spmd.clone, body=%wide.region_16.20_spmd.clone.sunk | while | flops 2423583744 | bytes 17480380 | solution.py:204
  362.7 6.0 fusion.161
  369.1 1.6 select_reduce_fusion.5
  372.6 6.0 fusion.161
  379.1 1.6 select_reduce_fusion.5
  382.6 6.0 fusion.161
  389.0 1.6 select_reduce_fusion.5
  392.5 6.0 fusion.161
  399.0 1.6 select_reduce_fusion.5
  402.5 6.0 fusion.161
  408.9 1.6 select_reduce_fusion.5
  412.4 6.0 fusion.161
  418.9 1.6 select_reduce_fusion.5
  422.4 6.0 fusion.161
  428.8 1.6 select_reduce_fusion.5
  432.3 6.0 fusion.161
  438.8 1.6 select_reduce_fusion.5
  442.4 40.9 %all-gather.11.cloned.1.call-done = f32[32,2,4096]{2,1,0:T(2,128)} async-done(((f32[1,2,4096]{2,1,0:T(2,128)}), f32[32,2,4096]{2,1,0:T(2,128)}) %all-gather.11.cloned.1.call-update) | async-done | bytes 1048592 | tf_op jit(solution)/shard_map/all_gather | solution.py:21
  484.0 43.5 %all-gather.9.cloned.1.call-done = f32[32,2,4096]{2,1,0:T(2,128)} async-done(((f32[1,2,4096]{2,1,0:T(2,128)}), f32[32,2,4096]{2,1,0:T(2,128)}) %all-gather.9.cloned.1.call-update) | async-done | bytes 1048592 | tf_op jit(solution)/shard_map/all_gather | solution.py:21
  528.2 43.4 %all-gather.7.cloned.1.call-done = f32[32,2,4096]{2,1,0:T(2,128)} async-done(((f32[1,2,4096]{2,1,0:T(2,128)}), f32[32,2,4096]{2,1,0:T(2,128)}) %all-gather.7.cloned.1.call-update) | async-done | bytes 1048592 | tf_op jit(solution)/shard_map/all_gather | solution.py:21
  572.4 27.7 %while.34 = (s32[]{:T(128)}, f32[2,4096]{1,0:T(2,128)S(1)}, f32[2,4096]{1,0:T(2,128)S(1)}, f32[2,4096]{1,0:T(2,128)S(1)}, f32[32,2,4096]{2,1,0:T(2,128)}, /*inde...) while((s32[]{:T(128)}, f32[2,4096]{1,0:T(2,128)S(1)}, ...), condition=%wide.region_22.23_spmd, body=%wide.region_21.22_spmd.sunk | while | flops 57349 | bytes 295059 | solution.py:27
  573.2 0.9 fusion.159
  574.1 0.9 fusion.159
  575.0 0.9 fusion.159
  575.9 0.9 fusion.159
  576.8 0.9 fusion.159
  577.7 0.9 fusion.159
  578.6 0.9 fusion.159
  579.5 0.9 fusion.159
  580.4 0.9 fusion.159
  584.0 0.9 fusion.159
  600.3 64.1 %all-reduce = f32[512]{0:T(512)S(1)} all-reduce(f32[512]{0:T(512)S(1)} %select_reduce_fusion.1), channel_id=2, replica_groups=mesh['req'=4,'exp'=32] {'req','exp'}, use_global_device_ids=true, to_apply=%region_25.26.clone | all-reduce | flops 512 | bytes 4096
  (179 shorter events, 46.2 us)
Async XLA Ops:
  7.2 177.5 %copy-start = (bf16[2,1,512,1024]{3,2,1,0:T(8,128)(2,1)S(1)}, bf16[2,1,512,1024]{3,2,1,0:T(8,128)(2,1)}, u32[]{:S(2)}) copy-start(bf16[2,1,512,1024]{3,2,1,0:T(8,128)(2,1)} %param.26) | copy-start | bytes 6291460
  9.3 5.2 copy-start.21
  12.4 1.0 copy-start.2
  14.9 0.6 copy-start.15
  24.7 1.0 copy-start.3
  25.7 6.6 copy-start.11
  25.7 7.2 %copy-start.8 = (s32[2,128,8]{1,2,0:T(8,128)S(1)}, s32[2,128,8]{1,2,0:T(8,128)}, u32[]{:S(2)}) copy-start(s32[2,128,8]{1,2,0:T(8,128)} %param.19) | copy-start | bytes 24580
  31.3 8.2 %copy-start.4 = (bf16[2,128,1024]{2,1,0:T(8,128)(2,1)S(1)}, bf16[2,128,1024]{2,1,0:T(8,128)(2,1)}, u32[]{:S(2)}) copy-start(bf16[2,128,1024]{2,1,0:T(8,128)(2,1)} %param.16) | copy-start | bytes 1572868
  39.4 5.0 copy-start.5
  41.6 5.9 copy-start.13
  63.3 5.6 copy-start.7
  63.3 24.2 %copy-start.6 = (s32[2,1024]{1,0:T(2,128)S(1)}, s32[2,1024]{1,0:T(2,128)}, u32[]{:S(2)}) copy-start(s32[2,1024]{1,0:T(2,128)} %eq.95) | copy-start | bytes 24580
  63.3 24.3 %copy-start.9 = (s32[2,128,8]{1,2,0:T(8,128)S(1)}, s32[2,128,8]{1,2,0:T(8,128)}, u32[]{:S(2)}) copy-start(s32[2,128,8]{1,2,0:T(8,128)} %broadcast_multiply_fusion.1) | copy-start | bytes 24580
  63.3 24.6 %copy-start.18 = (s32[2]{0:T(128)S(1)}, s32[2]{0:T(128)}, u32[]{:S(2)}) copy-start(s32[2]{0:T(128)} %iota_multiply_fusion) | copy-start | bytes 28
  105.0 71.5 %copy-start.20 = (bf16[2,1,1024,1024]{3,2,1,0:T(8,128)(2,1)S(1)}, bf16[2,1,1024,1024]{3,2,1,0:T(8,128)(2,1)}, u32[]{:S(2)}) copy-start(bf16[2,1,1024,1024]{3,2,1,0:T(8,128)(2,1)} %param.25) | copy-start | bytes 12582916
  195.0 5.0 copy-start.14
  195.0 66.9 %all-to-all-start.1 = ((bf16[2,32,40,1024]{3,2,0,1:T(8,128)(2,1)}), bf16[2,32,40,1024]{3,2,0,1:T(8,128)(2,1)}, u32[]{:S(2)}, u32[]{:S(2)}) async-start(bf16[2,32,40,1024]{3,2,0,1:T(8,128)(2,1)} %copy.129), calls=%async_computation.1 | async-start | bytes 10485760 | tf_op jit(solution)/shard_map/all_to_all | solution.py:166
  200.0 161.4 %all-gather.5.cloned.1.call-start = ((), (), s32[]{:S(2)}) async-start(), calls=%async_computation.2 | async-start | bytes 17301504 | tf_op jit(solution)/shard_map/all_gather | solution.py:184
  281.6 6.2 copy-start.12
  287.7 195.5 %all-gather.11.cloned.1.call-start = ((), (), s32[]{:S(2)}) async-start(), calls=%async_computation.5 | async-start | bytes 1081344 | tf_op jit(solution)/shard_map/all_gather | solution.py:21
  361.4 238.7 %copy-start.16 = (s32[128]{0:T(128)S(1)}, s32[128]{0:T(128)}, u32[]{:S(2)}) copy-start(s32[128]{0:T(128)} %copy-done.15) | copy-start | bytes 1540
  361.4 238.8 %copy-start.19 = (s32[4]{0:T(128)S(1)}, s32[4]{0:T(128)}, u32[]{:S(2)}) copy-start(s32[4]{0:T(128)} %param.21) | copy-start | bytes 52
  441.0 0.8 copy-start.10
  441.0 224.0 %copy-start.1 = (bf16[2,1,512,1024]{3,2,1,0:T(8,128)(2,1)S(1)}, bf16[2,1,512,1024]{3,2,1,0:T(8,128)(2,1)}, u32[]{:S(2)}) copy-start(bf16[2,1,512,1024]{3,2,1,0:T(8,128)(2,1)} %param.26) | copy-start | bytes 6291460
  441.0 86.4 %all-gather.9.cloned.1.call-start = ((), (), s32[]{:S(2)}) async-start(), calls=%async_computation.4 | async-start | bytes 1081344 | tf_op jit(solution)/shard_map/all_gather | solution.py:21
  441.8 129.8 %all-gather.7.cloned.1.call-start = ((), (), s32[]{:S(2)}) async-start(), calls=%async_computation.3 | async-start | bytes 1081344 | tf_op jit(solution)/shard_map/all_gather | solution.py:21
  600.1 65.0 %copy-start.17 = (f32[2,128]{1,0:T(2,128)}, f32[2,128]{1,0:T(2,128)S(1)}, u32[]{:S(2)}) copy-start(f32[2,128]{1,0:T(2,128)S(1)} %add_subtract_fusion) | copy-start | bytes 3076
Sparse Core Ops, SparseCore 0:
  287.8 73.5 all-gather.4
  441.2 42.0 all-gather.10
  485.5 41.9 all-gather.8
  529.6 41.9 all-gather.6
where the time goes:
time: 675 us; the launch traced here: 672 us
  waiting for transfers between devices  264 us (39%)
  blocking collectives  136 us (20%)
  matrix products  88 us (13%)
  local copies, waits for them, and re-layouts  84.9 us (13%)
  other arithmetic  73.5 us (11%)
  between operations  14.3 us (2%)
    all_gather x3, waiting for transfers between devices, combined_all(): everything = jax.tree.map(lambda part: lax.all_gather(part, axis), x)  128 us
    all_gather x1, waiting for transfers between devices, per_device(): shard_piece = lax.all_gather(final, 'exp', axis=1, tiled=True)  73.6 us
    all_to_all x1, blocking collectives, per_device(): lax.all_to_all(outgoing.reshape(2, groups, local_count * CAP, width), 'ex...  71.5 us
    unnamed x1, blocking collectives  64.1 us
    all_to_all x1, waiting for transfers between devices, per_device(): lax.all_to_all(produced.reshape(2, groups, local_count * CAP, width), 'ex...  61.7 us
    dot_general x8, matrix products, one_block(): jnp.einsum('mtd,mvd->mtv', row_block, vocab_head, preferred_element_type=...  47.9 us
    add x31, other arithmetic, join_parts(): first_mass * jnp.exp(first_max - joined_max)  27.2 us
    gather x2, local copies, waits for them, and re-layouts, per_device(): moe_in[:, token_index].reshape(-1, width)  21.3 us
  transfers between devices with their start and end apart: 5, of which 5 were waited for; matrix products, arithmetic and copies ran while one was open for 0% of the time, Pallas kernels for 0%

commit v1 on v0

--- a/solution.py
+++ b/solution.py
@@ -163,13 +163,11 @@
     produced = jnp.einsum(
         "mslcf,mlfd->mslcd", hidden, expert_down, preferred_element_type=jnp.float32
     ).astype(jnp.bfloat16)
-    returned = lax.all_to_all(
-        produced.reshape(2, groups, local_count * CAP, width),
-        "exp",
-        split_axis=1,
-        concat_axis=1,
-        tiled=True,
-    )
+    local = produced.reshape(2, groups, local_count * CAP, width)
+    h_now = jnp.split(local, jax.lax.axis_size("exp"), 1)
+    a_next = jnp.stack(h_now, axis=0)
+    local_out = jax.lax.all_to_all(a_next, split_axis=0, axis_name="exp", concat_axis=0)
+    returned = jnp.concatenate(local_out, 1)
     picked = returned.reshape(2 * EXPERTS * CAP, width)[slot_index].reshape(
         2, token_count, TOP, width
     )

time: 675 us -> 693 us (1.027)
  local copies, waits for them, and re-layouts: 84.9 us -> 103 us
    unnamed x50 -> x81, local copies, waits for them, and re-layouts: 3.31 us -> 24.3 us
where the time goes in v1:
time: 693 us; the launch traced here: 690 us
  waiting for transfers between devices  264 us (38%)
  blocking collectives  136 us (20%)
  local copies, waits for them, and re-layouts  103 us (15%)
  matrix products  88 us (13%)
  other arithmetic  73.5 us (11%)
  between operations  14.3 us (2%)
    all_gather x3, waiting for transfers between devices, combined_all(): everything = jax.tree.map(lambda part: lax.all_gather(part, axis), x)  128 us
    all_gather x1, waiting for transfers between devices, per_device(): shard_piece = lax.all_gather(final, 'exp', axis=1, tiled=True)  73.6 us
    all_to_all x1, blocking collectives, per_device(): lax.all_to_all(outgoing.reshape(2, groups, local_count * CAP, width), 'ex...  71.5 us
    unnamed x1, blocking collectives  64.1 us
    all_to_all x1, waiting for transfers between devices, per_device(): jax.lax.all_to_all(a_next, split_axis=0, axis_name='exp', concat_axis=0)  61.7 us
    dot_general x8, matrix products, one_block(): jnp.einsum('mtd,mvd->mtv', row_block, vocab_head, preferred_element_type=...  47.9 us
    add x31, other arithmetic, join_parts(): first_mass * jnp.exp(first_max - joined_max)  27.2 us
    unnamed x81, local copies, waits for them, and re-layouts  24.3 us
  transfers between devices with their start and end apart: 5, of which 5 were waited for; matrix products, arithmetic and copies ran while one was open for 0% of the time, Pallas kernels for 0%

profile of v1, /device:TPU:1, one launch (start us, length us, event | category | flops | bytes accessed | tf_op | source)
XLA Modules:
  0.0 690.0 jit_solution(15164467747743449619)
XLA Ops:
  7.2 1.4 fusion.72
  9.4 3.1 fusion.15
  12.5 1.0 copy-done.2
  15.6 2.3 fusion.42
  17.9 2.1 fusion.176
  20.0 1.6 slice.227
  21.6 3.1 fusion.13
  24.7 0.9 copy-done.3
  26.8 2.4 fusion.40
  29.2 2.1 fusion.171
  31.2 1.0 slice.226
  35.5 1.0 copy.264
  36.7 2.7 convolution_convert_fusion.2
  39.5 2.2 fusion.61
  41.6 2.8 convolution_convert_fusion.1
  44.4 2.2 fusion.64
  47.5 15.8 %gather_fusion = bf16[1024,2,1024]{2,1,0:T(2,128)(2,1)} fusion(bf16[2,128,1024]{2,0,1:T(2,128)(2,1)S(1)} %copy.280, s32[1024]{0:T(1024)S(1)} %broadcast_clamp_fusion.1), kind=kCustom, calls=%fused_computation | custom fusion | bytes 8392704 | tf_op jit(solution)/shard_map/gather | solution.py:151
  63.3 5.6 copy.281
  68.9 18.0 %reduce-window.11 = s32[2,32,8,128]{3,2,1,0:T(8,128)S(1)} reduce-window(s32[2,32,8,128]{3,2,1,0:T(8,128)S(1)} %fusion.101, s32[]{:T(128)} %constant.119.clone.1), window={size=1x1x1x128 pad=0_0x0_0x0_0x127_0}, to_apply=%region_9.10 | reduce-window | flops 8323072 | bytes 524292 | tf_op jit(solution)/shard_map/reduce-window.1
  88.0 13.6 %scatter_custom_fusion = bf16[2560,1024]{1,0:T(8,128)(2,1)} fusion(s32[2048]{0:T(1024)S(1)} %bitcast.453, bf16[2048,1024]{1,0:T(8,128)(2,1)} %bitcast.431, bf16[]{:T(256)} %constant.129.clone.1), kind=kCustom, calls=%fused_computation.37 | custom fusion | bytes 5243392 | tf_op jit(solution)/shard_map/scatter | solution.py:151
  101.7 3.3 copy.282
  105.0 71.5 %all_to_all.10 = bf16[2,32,40,1024]{3,2,0,1:T(8,128)(2,1)S(1)} all-to-all(bf16[2,32,40,1024]{3,2,0,1:T(8,128)(2,1)S(1)} %copy.282), channel_id=1, replica_groups=mesh['req'=4,'exp'=32] {'exp'}, dimensions={1} | all-to-all | bytes 10485760 | tf_op jit(solution)/shard_map/all_to_all | solution.py:153
  176.5 8.2 %fusion.19 = f32[2,32,1,40,1024]{4,3,1,0,2:T(8,128)} fusion(bf16[2,1,1024,1024]{3,2,1,0:T(8,128)(2,1)S(1)} %copy-done.20, bf16[2,32,40,1024]{3,2,0,1:T(8,128)(2,1)S(1)} %all_to_all.10), kind=kOutput, calls=%fused_computation.34 | convolution fusion | flops 5368709120 | bytes 19922944 | tf_op jit(solution)/shard_map/mslcd,mldf->mslcf/dot_general | solution.py:161
  184.7 7.2 %convolution_convert_fusion = bf16[2,32,40,1024]{3,2,1,0:T(8,128)(2,1)S(1)} fusion(f32[2,32,1,40,1024]{4,3,1,0,2:T(8,128)} %fusion.19, bf16[2,1,512,1024]{3,2,1,0:T(8,128)(2,1)S(1)} %copy-done), kind=kOutput, calls=%fused_computation.35 | convolution fusion | flops 2694840320 | bytes 17825792 | tf_op jit(solution)/shard_map/mslcf,mlfd->mslcd/dot_general | solution.py:163
  213.5 5.0 all-to-all-start.1
  218.7 61.7 %all-to-all-done.1 = bf16[32,2,1,40,1024]{4,3,1,2,0:T(8,128)(2,1)} async-done(((bf16[32,2,1,40,1024]{4,3,1,2,0:T(8,128)(2,1)}), bf16[32,2,1,40,1024]{4,3,1,2,0:T(8,128)(2,1)}, u32[]{:S(2)}, u32[]{:S(2)}) %all-to-all-start.1) | async-done | bytes 5242912 | tf_op jit(solution)/shard_map/all_to_all | solution.py:169
  280.4 5.6 copy.315
  286.0 14.1 %gather_fusion.1 = bf16[2048,1024]{1,0:T(8,128)(2,1)} fusion(bf16[2560,1024]{1,0:T(8,128)(2,1)} %bitcast.422, s32[2048]{0:T(1024)S(1)} %broadcast_clamp_fusion), kind=kCustom, calls=%fused_computation.1 | custom fusion | bytes 8396800 | tf_op jit(solution)/shard_map/gather | solution.py:171
  300.1 4.8 fusion.8
  305.2 1.0 multiply_convert_fusion
  306.3 73.6 %all-gather.5.cloned.1.call-done = bf16[2,4096,1024]{2,1,0:T(8,128)(2,1)} async-done(((bf16[2,128,1024]{2,1,0:T(8,128)(2,1)}), bf16[2,4096,1024]{2,1,0:T(8,128)(2,1)}) %all-gather.5.cloned.1.call-update) | async-done | bytes 16777232 | tf_op jit(solution)/shard_map/all_gather | solution.py:182
  379.9 79.6 %while.35 = (s32[]{:T(128)}, f32[8,2,512]{2,1,0:T(2,128)S(1)}, f32[8,2,512]{2,1,0:T(2,128)}, f32[8,2,512]{2,1,0:T(2,128)}, s32[8]{0:T(128)S(1)}, /*index=5*/bf16...) while((s32[]{:T(128)}, f32[8,2,512]{2,1,0:T(2,128)S(1)}, ...), condition=%wide.region_20.21_spmd.clone, body=%wide.region_16.20_spmd.clone.sunk | while | flops 2423583744 | bytes 17480380 | solution.py:202
  381.1 6.0 fusion.193
  387.6 1.6 select_reduce_fusion.5
  391.1 6.0 fusion.193
  397.6 1.6 select_reduce_fusion.5
  401.0 6.0 fusion.193
  407.5 1.6 select_reduce_fusion.5
  411.0 6.0 fusion.193
  417.4 1.6 select_reduce_fusion.5
  420.9 6.0 fusion.193
  427.4 1.6 select_reduce_fusion.5
  430.9 6.0 fusion.193
  437.4 1.6 select_reduce_fusion.5
  440.8 6.0 fusion.193
  447.3 1.6 select_reduce_fusion.5
  450.8 6.0 fusion.193
  457.3 1.6 select_reduce_fusion.5
  460.8 40.9 %all-gather.11.cloned.1.call-done = f32[32,2,4096]{2,1,0:T(2,128)} async-done(((f32[1,2,4096]{2,1,0:T(2,128)}), f32[32,2,4096]{2,1,0:T(2,128)}) %all-gather.11.cloned.1.call-update) | async-done | bytes 1048592 | tf_op jit(solution)/shard_map/all_gather | solution.py:21
  502.5 43.5 %all-gather.9.cloned.1.call-done = f32[32,2,4096]{2,1,0:T(2,128)} async-done(((f32[1,2,4096]{2,1,0:T(2,128)}), f32[32,2,4096]{2,1,0:T(2,128)}) %all-gather.9.cloned.1.call-update) | async-done | bytes 1048592 | tf_op jit(solution)/shard_map/all_gather | solution.py:21
  546.7 43.4 %all-gather.7.cloned.1.call-done = f32[32,2,4096]{2,1,0:T(2,128)} async-done(((f32[1,2,4096]{2,1,0:T(2,128)}), f32[32,2,4096]{2,1,0:T(2,128)}) %all-gather.7.cloned.1.call-update) | async-done | bytes 1048592 | tf_op jit(solution)/shard_map/all_gather | solution.py:21
  590.9 27.7 %while.34 = (s32[]{:T(128)}, f32[2,4096]{1,0:T(2,128)S(1)}, f32[2,4096]{1,0:T(2,128)S(1)}, f32[2,4096]{1,0:T(2,128)S(1)}, f32[32,2,4096]{2,1,0:T(2,128)}, /*inde...) while((s32[]{:T(128)}, f32[2,4096]{1,0:T(2,128)S(1)}, ...), condition=%wide.region_22.23_spmd, body=%wide.region_21.22_spmd.sunk | while | flops 57349 | bytes 295059 | solution.py:27
  591.7 0.9 fusion.191
  592.6 0.9 fusion.191
  593.5 0.9 fusion.191
  594.4 0.9 fusion.191
  595.3 0.9 fusion.191
  596.2 0.9 fusion.191
  597.1 0.9 fusion.191
  598.0 0.9 fusion.191
  598.9 0.9 fusion.191
  599.8 0.9 fusion.191
  605.1 0.9 fusion.191
  618.8 64.1 %all-reduce = f32[512]{0:T(512)S(1)} all-reduce(f32[512]{0:T(512)S(1)} %select_reduce_fusion.1), channel_id=2, replica_groups=mesh['req'=4,'exp'=32] {'req','exp'}, use_global_device_ids=true, to_apply=%region_25.26.clone | all-reduce | flops 512 | bytes 4096
  (210 shorter events, 67.0 us)
Async XLA Ops:
  7.2 177.5 %copy-start = (bf16[2,1,512,1024]{3,2,1,0:T(8,128)(2,1)S(1)}, bf16[2,1,512,1024]{3,2,1,0:T(8,128)(2,1)}, u32[]{:S(2)}) copy-start(bf16[2,1,512,1024]{3,2,1,0:T(8,128)(2,1)} %param.26) | copy-start | bytes 6291460
  9.3 5.2 copy-start.21
  12.4 1.0 copy-start.2
  14.9 0.6 copy-start.15
  24.7 1.0 copy-start.3
  25.6 6.6 copy-start.11
  25.6 7.2 %copy-start.8 = (s32[2,128,8]{1,2,0:T(8,128)S(1)}, s32[2,128,8]{1,2,0:T(8,128)}, u32[]{:S(2)}) copy-start(s32[2,128,8]{1,2,0:T(8,128)} %param.19) | copy-start | bytes 24580
  31.2 8.2 %copy-start.4 = (bf16[2,128,1024]{2,1,0:T(8,128)(2,1)S(1)}, bf16[2,128,1024]{2,1,0:T(8,128)(2,1)}, u32[]{:S(2)}) copy-start(bf16[2,128,1024]{2,1,0:T(8,128)(2,1)} %param.16) | copy-start | bytes 1572868
  36.7 7.7 %copy-start.5 = (bf16[2,128,1024]{2,1,0:T(8,128)(2,1)S(1)}, bf16[2,128,1024]{2,1,0:T(8,128)(2,1)}, u32[]{:S(2)}) copy-start(bf16[2,128,1024]{2,1,0:T(8,128)(2,1)} %param.16) | copy-start | bytes 1572868
  41.6 5.9 copy-start.13
  63.3 5.6 copy-start.7
  63.3 24.2 %copy-start.6 = (s32[2,1024]{1,0:T(2,128)S(1)}, s32[2,1024]{1,0:T(2,128)}, u32[]{:S(2)}) copy-start(s32[2,1024]{1,0:T(2,128)} %eq.95) | copy-start | bytes 24580
  63.3 24.3 %copy-start.9 = (s32[2,128,8]{1,2,0:T(8,128)S(1)}, s32[2,128,8]{1,2,0:T(8,128)}, u32[]{:S(2)}) copy-start(s32[2,128,8]{1,2,0:T(8,128)} %broadcast_multiply_fusion.1) | copy-start | bytes 24580
  63.3 24.6 %copy-start.18 = (s32[2]{0:T(128)S(1)}, s32[2]{0:T(128)}, u32[]{:S(2)}) copy-start(s32[2]{0:T(128)} %iota_multiply_fusion) | copy-start | bytes 28
  105.0 71.5 %copy-start.20 = (bf16[2,1,1024,1024]{3,2,1,0:T(8,128)(2,1)S(1)}, bf16[2,1,1024,1024]{3,2,1,0:T(8,128)(2,1)}, u32[]{:S(2)}) copy-start(bf16[2,1,1024,1024]{3,2,1,0:T(8,128)(2,1)} %param.25) | copy-start | bytes 12582916
  213.5 5.0 copy-start.14
  213.5 66.9 %all-to-all-start.1 = ((bf16[32,2,1,40,1024]{4,3,1,2,0:T(8,128)(2,1)}), bf16[32,2,1,40,1024]{4,3,1,2,0:T(8,128)(2,1)}, u32[]{:S(2)}, u32[]{:S(2)}) async-start(bf16[32,2,1,40,1024]{4,3,1,2,0:T(8,128)(2,1)} %fusion.104), calls=%async_computation.1 | async-start | bytes 10485760 | tf_op jit(solution)/shard_map/all_to_all | solution.py:169
  218.5 161.4 %all-gather.5.cloned.1.call-start = ((), (), s32[]{:S(2)}) async-start(), calls=%async_computation.2 | async-start | bytes 17301504 | tf_op jit(solution)/shard_map/all_gather | solution.py:182
  300.1 6.2 copy-start.12
  306.2 195.5 %all-gather.11.cloned.1.call-start = ((), (), s32[]{:S(2)}) async-start(), calls=%async_computation.5 | async-start | bytes 1081344 | tf_op jit(solution)/shard_map/all_gather | solution.py:21
  379.9 238.7 %copy-start.16 = (s32[128]{0:T(128)S(1)}, s32[128]{0:T(128)}, u32[]{:S(2)}) copy-start(s32[128]{0:T(128)} %copy-done.15) | copy-start | bytes 1540
  379.9 238.8 %copy-start.19 = (s32[4]{0:T(128)S(1)}, s32[4]{0:T(128)}, u32[]{:S(2)}) copy-start(s32[4]{0:T(128)} %param.21) | copy-start | bytes 52
  459.5 0.8 copy-start.10
  459.5 224.0 %copy-start.1 = (bf16[2,1,512,1024]{3,2,1,0:T(8,128)(2,1)S(1)}, bf16[2,1,512,1024]{3,2,1,0:T(8,128)(2,1)}, u32[]{:S(2)}) copy-start(bf16[2,1,512,1024]{3,2,1,0:T(8,128)(2,1)} %param.26) | copy-start | bytes 6291460
  459.5 86.5 %all-gather.9.cloned.1.call-start = ((), (), s32[]{:S(2)}) async-start(), calls=%async_computation.4 | async-start | bytes 1081344 | tf_op jit(solution)/shard_map/all_gather | solution.py:21
  460.3 129.8 %all-gather.7.cloned.1.call-start = ((), (), s32[]{:S(2)}) async-start(), calls=%async_computation.3 | async-start | bytes 1081344 | tf_op jit(solution)/shard_map/all_gather | solution.py:21
  618.5 65.0 %copy-start.17 = (f32[2,128]{1,0:T(2,128)}, f32[2,128]{1,0:T(2,128)S(1)}, u32[]{:S(2)}) copy-start(f32[2,128]{1,0:T(2,128)S(1)} %add_subtract_fusion) | copy-start | bytes 3076
Sparse Core Ops, SparseCore 0:
  306.3 73.5 all-gather.4
  459.6 42.0 all-gather.10
  504.0 41.9 all-gather.8
  548.1 41.9 all-gather.6
